TPU v7x, 32 devices: a whole 2x2x4 slice. The times are simulated.
32 devices in a mesh: grid: 4 (over z), mode: 8 (over y, x, core).
Axes of the slice: x: 2, y: 2, z: 4, core: 2. Of those that a mesh axis runs over, the one named last changes fastest.
Arguments:
- modes_field: bfloat16 [512, 192, 1024], P('mode', 'grid'), may hold values from -6 to 6
- chaos_basis: bfloat16 [512, 512], replicated, may hold values from -0.25 to 0.25
- node_weights: float32 [512], replicated, may hold values from 0.5 to 2
- node_points: float32 [512, 16], replicated, may hold values from -4 to 4
- kl_fields: float32 [16, 192, 1024], P(None, 'grid'), may hold values from -0.6 to 0.6
- velocity: float32 [2, 192, 1024], P(None, 'grid'), may hold values from -4 to 4
Outputs:
- tendency: bfloat16 [512, 192, 1024], P('mode', 'grid')
All inputs are finite; a program needn't handle non-finite values.
Results may differ from a plain program's by a relative error of at most 0.0053.
Values may be sent and summed in bfloat16 or wider, within the bound.
No kernel may reach another device: no remote copies, remote signals or barrier semaphores. Data moves between devices by JAX's collectives and lax.ppermute only.
A program may use at most 128 MiB of HBM per device.

v0:
```python
import jax
import jax.numpy as jnp
from jax import lax
from jax.sharding import PartitionSpec as P


def extended(cells, sides, width):
    for axis, dim in sides:
        count = lax.axis_size(axis)
        ends = count - 1
        head = lax.slice_in_dim(cells, 0, width, axis=dim)
        tail = lax.slice_in_dim(cells, cells.shape[dim] - width, cells.shape[dim], axis=dim)
        cells = jnp.concatenate(
            [
                lax.ppermute(tail, axis, [(i, (i + 1) % count) for i in range(ends)]),
                cells,
                lax.ppermute(head, axis, [((i + 1) % count, i) for i in range(ends)]),
            ],
            axis=dim,
        )
    return cells


def node_terms(padded_field, kl_piece, node_points, velocity_piece, node_weights):
    field_value = padded_field.astype(jnp.float32)
    viscosity = jnp.exp(
        jnp.einsum("qk,krc->qrc", node_points, kl_piece, precision=lax.Precision.HIGHEST)
    )
    center = field_value[:, 1:-1, 1:-1]
    visc_center = viscosity[:, 1:-1, 1:-1]

    def face_flux(near_field, near_visc):
        return 0.5 * (visc_center + near_visc) * (near_field - center)

    north = field_value[:, 2:, 1:-1]
    south = field_value[:, :-2, 1:-1]
    east = field_value[:, 1:-1, 2:]
    west = field_value[:, 1:-1, :-2]
    diffusion = face_flux(north, viscosity[:, 2:, 1:-1]) + face_flux(south, viscosity[:, :-2, 1:-1])
    diffusion = (
        diffusion
        + face_flux(east, viscosity[:, 1:-1, 2:])
        + face_flux(west, viscosity[:, 1:-1, :-2])
    )
    advection = 0.5 * velocity_piece[0] * (north - south) + 0.5 * velocity_piece[1] * (east - west)
    flux = diffusion - advection
    return (node_weights[:, None, None] * flux).astype(jnp.bfloat16)


def local(modes_field, chaos_basis, node_weights, node_points, kl_fields, velocity):
    kl_rimmed = extended(kl_fields, (("grid", 1),), 1)
    kl_rimmed = jnp.pad(kl_rimmed, ((0, 0), (0, 0), (1, 1)))
    result = jnp.einsum(
        "qp,prc->qrc",
        chaos_basis,
        lax.all_to_all(modes_field, "mode", split_axis=2, concat_axis=0, tiled=True),
        preferred_element_type=jnp.float32,
    )
    nodal = result.astype(jnp.bfloat16)
    node_blocks = lax.all_to_all(nodal, "mode", split_axis=0, concat_axis=2, tiled=True)
    rimmed = extended(node_blocks, (("grid", 1),), 1)
    padded_field = jnp.pad(rimmed, ((0, 0), (0, 0), (1, 1)))
    node_share = node_blocks.shape[0]
    first_index = lax.axis_index("mode") * node_share
    point_part = lax.dynamic_slice_in_dim(node_points, first_index, node_share, 0)
    weight_part = lax.dynamic_slice_in_dim(node_weights, first_index, node_share, 0)
    weighted = node_terms(padded_field, kl_rimmed, point_part, velocity, weight_part)
    cell_terms = lax.all_to_all(weighted, "mode", split_axis=2, concat_axis=0, tiled=True)
    tendency = jnp.einsum(
        "qp,qrc->prc", chaos_basis, cell_terms, preferred_element_type=jnp.float32
    )
    tendency = tendency.astype(jnp.bfloat16)
    return lax.all_to_all(tendency, "mode", split_axis=0, concat_axis=2, tiled=True)


def solution(mesh):
    return jax.shard_map(
        local,
        mesh=mesh,
        in_specs=(
            P("mode", "grid", None),
            P(),
            P(),
            P(),
            P(None, "grid", None),
            P(None, "grid", None),
        ),
        out_specs=P("mode", "grid", None),
        check_vma=False,
    )
```

profile of v0, /device:TPU:0, one launch (start us, length us, event | category | flops | bytes accessed | tf_op | source)
XLA Modules:
  0.0 571.1 jit_solution(2297330801579381977)
XLA Ops:
  0.0 0.0 copy-start
  0.0 20.8 %copy.58 = bf16[64,48,1024]{0,1,2:T(8,128)(2,1)} copy(bf16[64,48,1024]{2,1,0:T(8,128)(2,1)} %param.6) | data formatting | bytes 12582912 | tf_op args[0]
  20.8 13.7 %reshape.3 = bf16[8,2,196608]{2,1,0:T(2,128)(2,1)} reshape(bf16[1024,48,64]{2,1,0:T(8,128)(2,1)} %bitcast.48) | data formatting | bytes 12582912
  34.5 77.6 %all_to_all.72 = bf16[8,2,196608]{2,1,0:T(2,128)(2,1)} all-to-all(bf16[8,2,196608]{2,1,0:T(2,128)(2,1)} %reshape.3), channel_id=1, replica_groups=mesh['grid'=4,'mode'=8] {'mode'}, dimensions={0} | all-to-all | bytes 12582912 | tf_op jit(solution)/shard_map/all_to_all | solution.py:56
  112.1 13.3 %reshape.4 = bf16[1024,48,64]{2,1,0:T(8,128)(2,1)} reshape(bf16[8,2,196608]{2,1,0:T(2,128)(2,1)} %all_to_all.72) | data formatting | bytes 12582912
  125.4 14.1 %copy.59 = bf16[64,48,8,128]{3,0,2,1:T(8,128)(2,1)} copy(bf16[64,48,8,128]{0,1,3,2:T(8,128)(2,1)} %bitcast.45) | data formatting | bytes 12582912 | tf_op jit(solution)/shard_map/all_to_all | solution.py:56
  139.5 0.0 copy-done
  139.5 6.4 %convolution_convert_fusion = bf16[512,48,128]{2,0,1:T(8,128)(2,1)S(1)} fusion(bf16[512,48,128]{2,0,1:T(8,128)(2,1)} %bitcast.54, bf16[512,512]{1,0:T(8,128)(2,1)S(1)} %copy-done), kind=kOutput, calls=%fused_computation.40 | convolution fusion | flops 3224371200 | bytes 13107200 | tf_op jit(solution)/shard_map/qp,prc->qrc/dot_general | solution.py:53
  145.9 6.8 %copy.60 = bf16[512,48,128]{2,1,0:T(8,128)(2,1)} copy(bf16[512,48,128]{2,0,1:T(8,128)(2,1)S(1)} %convolution_convert_fusion) | data formatting | bytes 12582912 | tf_op jit(solution)/shard_map/convert_element_type | solution.py:59
  152.7 0.0 copy-start.2
  152.7 5.1 all-to-all-start.1
  157.8 3.7 copy.55
  161.5 0.0 copy-start.1
  161.5 1.7 copy-done.1
  163.2 4.3 collective-permute-start
  167.5 1.3 collective-permute-start.1
  168.8 0.8 dynamic_slice.6
  169.5 0.0 copy-done.2
  169.6 59.6 %all-to-all-done.1 = bf16[512,48,128]{2,1,0:T(8,128)(2,1)} async-done(((bf16[512,48,128]{2,1,0:T(8,128)(2,1)}), bf16[512,48,128]{2,1,0:T(8,128)(2,1)}, u32[]{:S(2)}, u32[]{:S(2)}) %all-to-all-start.1) | async-done | bytes 6291488 | tf_op jit(solution)/shard_map/all_to_all | solution.py:60
  229.2 9.5 %copy.75 = bf16[8,64,48,128]{3,0,1,2:T(8,128)(2,1)} copy(bf16[8,64,48,128]{3,2,1,0:T(8,128)(2,1)} %bitcast.5) | data formatting | bytes 12582912 | tf_op jit(solution)/shard_map/all_to_all | solution.py:60
  238.7 10.3 %all_to_all.59 = bf16[64,48,1024]{2,0,1:T(8,128)(2,1)} reshape(bf16[64,48,8,128]{3,2,0,1:T(8,128)(2,1)} %bitcast.51) | data formatting | bytes 12582912 | tf_op jit(solution)/shard_map/all_to_all | solution.py:60
  249.0 0.0 slice-start
  249.0 1.1 fusion.39
  250.2 4.4 collective-permute-start.2
  254.6 0.0 slice-start.1
  254.6 1.6 collective-permute-start.3
  256.2 0.0 collective-permute-done
  256.2 0.0 collective-permute-done.1
  256.2 16.3 %convolution_exponential_fusion = f32[64,50,1026]{2,0,1:T(8,128)} fusion(f32[16,1,1024]{2,0,1:T(8,128)S(1)} %collective-permute-done.1, f32[16,48,1024]{2,0,1:T(8,128)} %copy-done.1, f32[16,1,1024]{2,0,1:T(8,128)S(1)} %collective-permute-done, f32[512,16]{0,1:T(8,128)} %param.9, s32[]{:T(128)S(6)} %select_n.4), kind=kOutput, calls=%fused_computation.2 | convolution fusion | flops 636940800 | bytes 16417796 | tf_op jit(solution)/shard_map/qk,krc->qrc/dot_general | solution.py:27
  272.5 0.0 collective-permute-done.2
  272.5 0.0 collective-permute-done.3
  272.5 0.0 slice-done
  272.5 0.0 slice-done.1
  272.5 7.0 %fusion.20 = f32[64,50,1026]{2,0,1:T(8,128)} fusion(bf16[64,1,1024]{2,0,1:T(8,128)(2,1)S(1)} %collective-permute-done.3, bf16[64,48,1024]{2,0,1:T(8,128)(2,1)S(1)} %bitcast.50, bf16[64,1,1024]{2,0,1:T(8,128)(2,1)S(1)} %collective-permute-done.2), kind=kLoop, calls=%fused_computation.27 | loop fusion | flops 39398400 | bytes 19686400 | tf_op jit(solution)/shard_map/convert_element_type | solution.py:25
  279.5 60.8 %fusion.6 = bf16[64,48,1024]{2,0,1:T(8,128)(2,1)} fusion(f32[64,50,1026]{2,0,1:T(8,128)} %convolution_exponential_fusion, f32[64,50,1026]{2,0,1:T(8,128)} %fusion.20, f32[48,1024]{1,0:T(8,128)S(1)} %get-tuple-element.10, f32[48,1024]{1,0:T(8,128)S(1)} %get-tuple-element.9, f32[64]{0:T(128)S(1)} %dynamic_slice.6), kind=kLoop, calls=%fused_computation.10 | loop fusion | flops 84934656 | bytes 132514048 | tf_op jit(solution)/shard_map/convert_element_type | solution.py:47
  340.4 15.7 %copy.62 = bf16[64,48,1024]{0,1,2:T(8,128)(2,1)} copy(bf16[64,48,1024]{2,0,1:T(8,128)(2,1)} %fusion.6) | data formatting | bytes 12582912 | tf_op jit(solution)/shard_map/convert_element_type | solution.py:47
  356.1 13.7 %reshape.5 = bf16[8,2,196608]{2,1,0:T(2,128)(2,1)} reshape(bf16[1024,48,64]{2,1,0:T(8,128)(2,1)} %bitcast.46) | data formatting | bytes 12582912
  369.8 76.9 %all_to_all.73 = bf16[8,2,196608]{2,1,0:T(2,128)(2,1)} all-to-all(bf16[8,2,196608]{2,1,0:T(2,128)(2,1)} %reshape.5), channel_id=1, replica_groups=mesh['grid'=4,'mode'=8] {'mode'}, dimensions={0} | all-to-all | bytes 12582912 | tf_op jit(solution)/shard_map/all_to_all | solution.py:68
  446.7 13.3 %reshape.6 = bf16[1024,48,64]{2,1,0:T(8,128)(2,1)} reshape(bf16[8,2,196608]{2,1,0:T(2,128)(2,1)} %all_to_all.73) | data formatting | bytes 12582912
  460.0 14.1 %copy.70 = bf16[8,64,48,128]{3,1,0,2:T(8,128)(2,1)} copy(bf16[8,64,48,128]{1,2,3,0:T(8,128)(2,1)} %bitcast.47) | data formatting | bytes 12582912 | tf_op jit(solution)/shard_map/all_to_all | solution.py:68
  474.1 8.2 %convert_bitcast_fusion = bf16[512,48,128]{0,2,1:T(8,128)(2,1)} fusion(bf16[512,48,128]{2,0,1:T(8,128)(2,1)} %bitcast.53, bf16[512,512]{1,0:T(8,128)(2,1)S(1)} %copy-done), kind=kOutput, calls=%fused_computation.30 | convolution fusion | flops 3224371200 | bytes 13107200 | tf_op jit(solution)/shard_map/qp,qrc->prc/dot_general | solution.py:69
  482.4 9.0 %copy.66 = bf16[512,48,128]{2,1,0:T(8,128)(2,1)} copy(bf16[512,48,128]{0,2,1:T(8,128)(2,1)} %convert_bitcast_fusion) | data formatting | bytes 12582912 | tf_op jit(solution)/shard_map/convert_element_type | solution.py:72
  491.3 75.2 %all_to_all.74 = bf16[512,48,128]{2,1,0:T(8,128)(2,1)S(1)} all-to-all(bf16[512,48,128]{2,1,0:T(8,128)(2,1)} %copy.66), channel_id=1, replica_groups=mesh['grid'=4,'mode'=8] {'mode'}, dimensions={0} | all-to-all | bytes 12582912 | tf_op jit(solution)/shard_map/all_to_all | solution.py:73
  566.5 4.5 copy.74
  (3 shorter events, 0.0 us)
Async XLA Ops:
  0.0 139.5 %copy-start = (bf16[512,512]{1,0:T(8,128)(2,1)S(1)}, bf16[512,512]{1,0:T(8,128)(2,1)}, u32[]{:S(2)}) copy-start(bf16[512,512]{1,0:T(8,128)(2,1)} %param.7) | copy-start | bytes 1572868
  152.7 16.8 %copy-start.2 = (f32[2,48,1024]{2,1,0:T(8,128)S(1)}, f32[2,48,1024]{2,1,0:T(8,128)}, u32[]{:S(2)}) copy-start(f32[2,48,1024]{2,1,0:T(8,128)} %param.11) | copy-start | bytes 1179652
  152.7 76.5 %all-to-all-start.1 = ((bf16[512,48,128]{2,1,0:T(8,128)(2,1)}), bf16[512,48,128]{2,1,0:T(8,128)(2,1)}, u32[]{:S(2)}, u32[]{:S(2)}) async-start(bf16[512,48,128]{2,1,0:T(8,128)(2,1)} %copy.60), calls=%async_computation.1 | async-start | bytes 12582912 | tf_op jit(solution)/shard_map/all_to_all | solution.py:60
  161.5 1.7 copy-start.1
  163.2 93.0 %collective-permute-start = (f32[16,1,1024]{2,0,1:T(8,128)S(1)}, f32[16,1,1024]{2,0,1:T(8,128)S(1)}, u32[]{:S(2)}, u32[]{:S(2)}) collective-permute-start(f32[16,1,1024]{2,0,1:T(8,128)S(1)} %get-tuple-element.7), channel_id=1, source_target_pairs={{0,8},{8,16},{16,24},{1,9},{9,17},{17,25},{2,10},{10,18},{18,26},{... | collective-permute-start | bytes 196616 | tf_op jit(solution)/shard_map/ppermute | solution.py:15
  167.5 88.8 %collective-permute-start.1 = (f32[16,1,1024]{2,0,1:T(8,128)S(1)}, f32[16,1,1024]{2,0,1:T(8,128)S(1)}, u32[]{:S(2)}, u32[]{:S(2)}) collective-permute-start(f32[16,1,1024]{2,0,1:T(8,128)S(1)} %get-tuple-element.8), channel_id=1, source_target_pairs={{8,0},{16,8},{24,16},{9,1},{17,9},{25,17},{10,2},{18,10},{26,18},{... | collective-permute-start | bytes 196616 | tf_op jit(solution)/shard_map/ppermute | solution.py:17
  249.0 23.5 %slice-start = ((s8[6291456]{0:T(1024)(128)(4,1)}), s8[4194304]{0:T(1024)(128)(4,1)S(1)}, s32[]{:S(2)}) async-start(s8[6291456]{0:T(1024)(128)(4,1)} %bitcast.49), calls=%async_computation.4 | async-start | bytes 8388608
  250.2 22.3 %collective-permute-start.2 = (bf16[64,1,1024]{2,0,1:T(8,128)(2,1)S(1)}, bf16[64,1,1024]{2,0,1:T(8,128)(2,1)S(1)}, u32[]{:S(2)}, u32[]{:S(2)}) collective-permute-start(bf16[64,1,1024]{2,0,1:T(8,128)(2,1)S(1)} %get-tuple-element.5), channel_id=1, source_target_pairs={{0,8},{8,16},{16,24},{1,9},{9,17},{17,25},{2,10},{10,18},{18,26},{... | collective-permute-start | bytes 393224 | tf_op jit(solution)/shard_map/ppermute | solution.py:15
  254.6 18.0 %slice-start.1 = ((s8[6291456]{0:T(1024)(128)(4,1)}), s8[2097152]{0:T(1024)(128)(4,1)S(1)}, s32[]{:S(2)}) async-start(s8[6291456]{0:T(1024)(128)(4,1)} %bitcast.49), calls=%async_computation.5 | async-start | bytes 4194304
  254.6 17.9 %collective-permute-start.3 = (bf16[64,1,1024]{2,0,1:T(8,128)(2,1)S(1)}, bf16[64,1,1024]{2,0,1:T(8,128)(2,1)S(1)}, u32[]{:S(2)}, u32[]{:S(2)}) collective-permute-start(bf16[64,1,1024]{2,0,1:T(8,128)(2,1)S(1)} %get-tuple-element.6), channel_id=1, source_target_pairs={{8,0},{16,8},{24,16},{9,1},{17,9},{25,17},{10,2},{18,10},{26,18},{... | collective-permute-start | bytes 393224 | tf_op jit(solution)/shard_map/ppermute | solution.py:17
where the time goes:
time: 574 us; the launch traced here: 571 us
  blocking collectives  230 us (40%)
  local copies, waits for them, and re-layouts  166 us (29%)
  other arithmetic  67.9 us (12%)
  waiting for transfers between devices  59.6 us (10%)
  matrix products  30.9 us (5%)
  starting transfers between devices  16.7 us (3%)
    unnamed x16, local copies, waits for them, and re-layouts  80.3 us
    all_to_all x1, blocking collectives, local(): lax.all_to_all(modes_field, 'mode', split_axis=2, concat_axis=0, tiled=True)  77.6 us
    all_to_all x1, blocking collectives, local(): lax.all_to_all(weighted, 'mode', split_axis=2, concat_axis=0, tiled=True)  76.9 us
    all_to_all x1, blocking collectives, local(): lax.all_to_all(tendency, 'mode', split_axis=0, concat_axis=2, tiled=True)  75.2 us
    convert_element_type x1, other arithmetic, node_terms(): return (node_weights[:, None, None] * flux).astype(jnp.bfloat16)  60.8 us
    all_to_all x1, waiting for transfers between devices, local(): lax.all_to_all(nodal, 'mode', split_axis=0, concat_axis=2, tiled=True)  59.6 us
    all_to_all x2, local copies, waits for them, and re-layouts, local(): lax.all_to_all(nodal, 'mode', split_axis=0, concat_axis=2, tiled=True)  19.8 us
    dot_general x1, matrix products, node_terms(): jnp.einsum('qk,krc->qrc', node_points, kl_piece, precision=lax.Precision....  16.3 us
  transfers between devices with their start and end apart: 5, of which 1 were waited for; matrix products, arithmetic and copies ran while one was open for 6% of the time, Pallas kernels for 0%

commit v1 on v0

--- a/solution.py
+++ b/solution.py
@@ -48,8 +48,12 @@
 
 
 def local(modes_field, chaos_basis, node_weights, node_points, kl_fields, velocity):
+    columns = modes_field.shape[2] // lax.axis_size("mode")
+    first_column = lax.axis_index("mode") * columns
     kl_rimmed = extended(kl_fields, (("grid", 1),), 1)
     kl_rimmed = jnp.pad(kl_rimmed, ((0, 0), (0, 0), (1, 1)))
+    kl_piece = lax.dynamic_slice_in_dim(kl_rimmed, first_column, columns + 2, 2)
+    velocity_piece = lax.dynamic_slice_in_dim(velocity, first_column, columns, 2)
     result = jnp.einsum(
         "qp,prc->qrc",
         chaos_basis,
@@ -57,17 +61,10 @@
         preferred_element_type=jnp.float32,
     )
     nodal = result.astype(jnp.bfloat16)
-    node_blocks = lax.all_to_all(nodal, "mode", split_axis=0, concat_axis=2, tiled=True)
-    rimmed = extended(node_blocks, (("grid", 1),), 1)
-    padded_field = jnp.pad(rimmed, ((0, 0), (0, 0), (1, 1)))
-    node_share = node_blocks.shape[0]
-    first_index = lax.axis_index("mode") * node_share
-    point_part = lax.dynamic_slice_in_dim(node_points, first_index, node_share, 0)
-    weight_part = lax.dynamic_slice_in_dim(node_weights, first_index, node_share, 0)
-    weighted = node_terms(padded_field, kl_rimmed, point_part, velocity, weight_part)
-    cell_terms = lax.all_to_all(weighted, "mode", split_axis=2, concat_axis=0, tiled=True)
+    padded_field = extended(nodal, (("mode", 2), ("grid", 1)), 1)
+    weighted = node_terms(padded_field, kl_piece, node_points, velocity_piece, node_weights)
     tendency = jnp.einsum(
-        "qp,qrc->prc", chaos_basis, cell_terms, preferred_element_type=jnp.float32
+        "qp,qrc->prc", chaos_basis, weighted, preferred_element_type=jnp.float32
     )
     tendency = tendency.astype(jnp.bfloat16)
     return lax.all_to_all(tendency, "mode", split_axis=0, concat_axis=2, tiled=True)

time: 574 us -> 346 us (0.60)
  blocking collectives: 230 us -> 77.8 us
  local copies, waits for them, and re-layouts: 166 us -> 94.7 us
  other arithmetic: 67.9 us -> 16.4 us
  matrix products: 30.9 us -> 73 us
    all_to_all x2 -> x0, blocking collectives: 154 us -> none  [the longest x1 77.6 us: local(): lax.all_to_all(modes_field, 'mode', split_axis=2, concat_axis=0, tiled=True)]
    convert_element_type x1, other arithmetic: 60.8 us -> 8.26 us  [local(): nodal = result.astype(jnp.bfloat16)]
    all_to_all x3 -> x0, local copies, waits for them, and re-layouts: 33.9 us -> none  [the longest x2 19.8 us: local(): lax.all_to_all(nodal, 'mode', split_axis=0, concat_axis=2, tiled=True)]
    dot_general x2 -> x1, matrix products: 14.6 us -> 46.6 us  [local(): jnp.einsum('qp,qrc->prc', chaos_basis, weighted, preferred_element_type=j...]
    unnamed x16 -> x18, local copies, waits for them, and re-layouts: 80.3 us -> 53.3 us
    convert_element_type x2 -> x0, local copies, waits for them, and re-layouts: 22.5 us -> none  [the longest x1 15.7 us: node_terms(): return (node_weights[:, None, None] * flux).astype(jnp.bfloat16)]
    all_to_all x1 -> x2, local copies, waits for them, and re-layouts: 14.1 us -> 26.3 us  [local(): lax.all_to_all(modes_field, 'mode', split_axis=2, concat_axis=0, tiled=True)]
    unnamed x0 -> x1, matrix products: none -> 9.32 us
  transfers between devices with their start and end apart: 5 -> 7, of which waited for: 1 -> 2; matrix products, arithmetic and copies ran while one was open for 6% -> 24% of each run, Pallas kernels for 0% -> 0%
where the time goes in v1:
time: 346 us; the launch traced here: 344 us
  local copies, waits for them, and re-layouts  94.7 us (27%)
  blocking collectives  77.8 us (22%)
  matrix products  73 us (21%)
  waiting for transfers between devices  62.4 us (18%)
  starting transfers between devices  19.7 us (6%)
  other arithmetic  16.4 us (5%)
    all_to_all x1, blocking collectives, local(): lax.all_to_all(tendency, 'mode', split_axis=0, concat_axis=2, tiled=True)  77.8 us
    all_to_all x1, waiting for transfers between devices, local(): lax.all_to_all(modes_field, 'mode', split_axis=2, concat_axis=0, tiled=True)  60.5 us
    unnamed x18, local copies, waits for them, and re-layouts  53.3 us
    dot_general x1, matrix products, local(): jnp.einsum('qp,qrc->prc', chaos_basis, weighted, preferred_element_type=j...  46.6 us
    all_to_all x2, local copies, waits for them, and re-layouts, local(): lax.all_to_all(modes_field, 'mode', split_axis=2, concat_axis=0, tiled=True)  26.3 us
    dot_general x1, matrix products, node_terms(): jnp.einsum('qk,krc->qrc', node_points, kl_piece, precision=lax.Precision....  17 us
    ppermute x3, starting transfers between devices, extended(): lax.ppermute(tail, axis, [(i, (i + 1) % count) for i in range(ends)])  10.2 us
    unnamed x1, matrix products  9.32 us
  transfers between devices with their start and end apart: 7, of which 2 were waited for; matrix products, arithmetic and copies ran while one was open for 24% of the time, Pallas kernels for 0%

profile of v1, /device:TPU:0, one launch (start us, length us, event | category | flops | bytes accessed | tf_op | source)
XLA Modules:
  0.0 344.2 jit_solution(16087460951043694542)
XLA Ops:
  0.0 0.0 copy-start
  0.0 20.8 %copy.36 = bf16[64,48,1024]{0,1,2:T(8,128)(2,1)} copy(bf16[64,48,1024]{2,1,0:T(8,128)(2,1)} %param.6) | data formatting | bytes 12582912 | tf_op args[0]
  20.8 13.7 %reshape.5 = bf16[8,2,196608]{2,1,0:T(2,128)(2,1)} reshape(bf16[1024,48,64]{2,1,0:T(8,128)(2,1)} %bitcast.38) | data formatting | bytes 12582912
  34.5 5.2 %all-to-all-start = ((bf16[8,2,196608]{2,1,0:T(2,128)(2,1)}), bf16[8,2,196608]{2,1,0:T(2,128)(2,1)}, u32[]{:S(2)}, u32[]{:S(2)}) async-start(bf16[8,2,196608]{2,1,0:T(2,128)(2,1)} %reshape.5), calls=%async_computation | async-start | bytes 12582912 | tf_op jit(solution)/shard_map/all_to_all | solution.py:60
  39.7 3.7 %copy.33 = f32[16,48,1024]{2,0,1:T(8,128)S(1)} copy(f32[16,48,1024]{2,1,0:T(8,128)} %param.10) | data formatting | bytes 6291456 | tf_op args[4]
  43.4 0.0 copy-start.2
  43.4 1.7 copy-done.2
  45.1 4.6 %collective-permute-start = (f32[16,1,1024]{2,0,1:T(8,128)S(1)}, f32[16,1,1024]{2,0,1:T(8,128)S(1)}, u32[]{:S(2)}, u32[]{:S(2)}) collective-permute-start(f32[16,1,1024]{2,0,1:T(8,128)S(1)} %get-tuple-element.10), channel_id=1, source_target_pairs={{0,8},{8,16},{16,24},{1,9},{9,17},{17,25},{2,10},{10,18},{18,26},{... | collective-permute-start | bytes 196616 | tf_op jit(solution)/shard_map/ppermute | solution.py:15
  49.7 1.3 collective-permute-start.1
  51.0 60.5 %all-to-all-done = bf16[8,2,196608]{2,1,0:T(2,128)(2,1)} async-done(((bf16[8,2,196608]{2,1,0:T(2,128)(2,1)}), bf16[8,2,196608]{2,1,0:T(2,128)(2,1)}, u32[]{:S(2)}, u32[]{:S(2)}) %all-to-all-start) | async-done | bytes 6291488 | tf_op jit(solution)/shard_map/all_to_all | solution.py:60
  111.5 13.3 %reshape.6 = bf16[1024,48,64]{2,1,0:T(8,128)(2,1)} reshape(bf16[8,2,196608]{2,1,0:T(2,128)(2,1)} %all-to-all-done) | data formatting | bytes 12582912
  124.8 17.2 %copy.38 = bf16[8,64,48,128]{3,2,1,0:T(8,128)(2,1)} copy(bf16[8,64,48,128]{1,2,3,0:T(8,128)(2,1)} %bitcast.37) | data formatting | bytes 12582912 | tf_op jit(solution)/shard_map/all_to_all | solution.py:60
  142.1 9.1 %copy.39 = bf16[512,48,128]{0,2,1:T(8,128)(2,1)} copy(bf16[512,48,128]{2,1,0:T(8,128)(2,1)} %bitcast.41) | data formatting | bytes 12582912 | tf_op jit(solution)/shard_map/all_to_all | solution.py:60
  151.2 0.0 copy-done
  151.2 9.3 %fusion.47 = f32[512,6144]{0,1} fusion(bf16[512,512]{1,0:T(8,128)(2,1)S(1)} %copy-done, bf16[512,6144]{0,1:T(8,128)(2,1)} %bitcast.39), kind=kOutput, calls=%fused_computation.56 | convolution fusion | flops 3221225472 | bytes 19398656
  160.5 0.0 copy-start.3
  160.5 8.3 %convert_element_type.17 = bf16[512,48,128]{0,2,1:T(8,128)(2,1)} convert(f32[512,48,128]{0,2,1:T(8,128)} %bitcast.34) | non-fusion elementwise | flops 3145728 | bytes 18874368 | tf_op jit(solution)/shard_map/convert_element_type | solution.py:63
  168.8 0.0 slice-start
  168.8 1.4 fusion.45
  170.2 1.3 collective-permute-start.2
  171.5 1.3 collective-permute-start.3
  172.8 0.8 fusion.38
  173.6 0.0 collective-permute-done.2
  173.6 1.8 collective-permute-done.3
  175.4 1.0 pad_maximum_fusion.2
  176.5 4.3 %collective-permute-start.4 = (bf16[512,1,130]{0,2,1:T(8,128)(2,1)S(1)}, bf16[512,1,130]{0,2,1:T(8,128)(2,1)S(1)}, u32[]{:S(2)}, u32[]{:S(2)}) collective-permute-start(bf16[512,1,130]{0,2,1:T(8,128)(2,1)S(1)} %get-tuple-element.5), channel_id=1, source_target_pairs={{0,8},{8,16},{16,24},{1,9},{9,17},{17,25},{2,10},{10,18},{18,26},{... | collective-permute-start | bytes 399368 | tf_op jit(solution)/shard_map/ppermute | solution.py:15
  180.8 0.0 slice-start.1
  180.8 1.7 collective-permute-start.5
  182.6 0.0 collective-permute-done
  182.6 0.0 collective-permute-done.1
  182.6 0.0 copy-done.3
  182.6 17.0 %exponential_bitcast_fusion = f32[512,50,130]{0,2,1:T(8,128)} fusion(s32[]{:T(128)S(6)} %select_n.6, f32[16,1,1024]{2,0,1:T(8,128)S(1)} %collective-permute-done, f32[16,48,1024]{2,0,1:T(8,128)} %copy-done.2, f32[16,1,1024]{2,0,1:T(8,128)S(1)} %collective-permute-done.1, f32[512,16]{0,1:T(8,128)S(1)} %copy-done.3), kind=kOutput, calls=%fused_computation | convolution fusion | flops 639912000 | bytes 16622592 | tf_op jit(solution)/shard_map/qk,krc->qrc/dot_general | solution.py:27
  199.6 0.0 copy-start.4
  199.6 0.0 collective-permute-done.4
  199.6 0.0 collective-permute-done.5
  199.6 0.0 slice-done
  199.7 0.0 slice-done.1
  199.7 6.3 %maximum_convert_fusion = f32[512,50,130]{0,2,1:T(8,128)} fusion(bf16[512,1,130]{0,2,1:T(8,128)(2,1)S(1)} %collective-permute-done.5, bf16[512,48,1]{0,2,1:T(2,128)(2,1)S(1)} %collective-permute-done.3, bf16[512,48,128]{0,2,1:T(8,128)(2,1)S(1)} %bitcast.36, bf16[512,48,1]{0,2,1:T(2,128)(2,1)S(1)} %collective-permute-done.2, ...), kind=kLoop, calls=%fused_computation.19 | loop fusion | flops 33280000 | bytes 19968000 | tf_op jit(solution)/shard_map/convert_element_type | solution.py:25
  206.0 0.0 copy-done.4
  206.0 46.6 %convert_bitcast_fusion = bf16[512,48,128]{0,2,1:T(8,128)(2,1)} fusion(f32[512,50,130]{0,2,1:T(8,128)} %exponential_bitcast_fusion, f32[512,50,130]{0,2,1:T(8,128)} %maximum_convert_fusion, f32[48,128]{1,0:T(8,128)S(1)} %get-tuple-element.12, f32[48,128]{1,0:T(8,128)S(1)} %get-tuple-element.11, f32[512]{0:T(512)S(1)} %copy-done.4, ...), kind=kOutput, calls=%fused_computation.21 | convolution fusion | flops 3309305856 | bytes 132696064 | tf_op jit(solution)/shard_map/qp,qrc->prc/dot_general | solution.py:66
  252.6 0.0 copy-start.1
  252.6 9.2 %copy.40 = bf16[512,48,128]{2,1,0:T(8,128)(2,1)} copy(bf16[512,48,128]{0,2,1:T(8,128)(2,1)} %convert_bitcast_fusion) | data formatting | bytes 12582912 | tf_op jit(solution)/shard_map/convert_element_type | solution.py:69
  261.8 77.8 %all_to_all.36 = bf16[512,48,128]{2,1,0:T(8,128)(2,1)S(1)} all-to-all(bf16[512,48,128]{2,1,0:T(8,128)(2,1)} %copy.40), channel_id=1, replica_groups=mesh['grid'=4,'mode'=8] {'mode'}, dimensions={0} | all-to-all | bytes 12582912 | tf_op jit(solution)/shard_map/all_to_all | solution.py:70
  339.6 4.5 %copy.46 = bf16[8,64,6,8,128]{4,3,0,2,1:T(8,128)(2,1)} copy(bf16[8,64,6,8,128]{4,3,2,1,0:T(8,128)(2,1)S(1)} %bitcast.40) | data formatting | bytes 12582912 | tf_op jit(solution)/shard_map/all_to_all | solution.py:70
  344.2 0.0 copy-done.1
  (2 shorter events, 0.0 us)
Async XLA Ops:
  0.0 151.2 %copy-start = (bf16[512,512]{1,0:T(8,128)(2,1)S(1)}, bf16[512,512]{1,0:T(8,128)(2,1)}, u32[]{:S(2)}) copy-start(bf16[512,512]{1,0:T(8,128)(2,1)} %param.7) | copy-start | bytes 1572868
  34.5 77.0 %all-to-all-start = ((bf16[8,2,196608]{2,1,0:T(2,128)(2,1)}), bf16[8,2,196608]{2,1,0:T(2,128)(2,1)}, u32[]{:S(2)}, u32[]{:S(2)}) async-start(bf16[8,2,196608]{2,1,0:T(2,128)(2,1)} %reshape.5), calls=%async_computation | async-start | bytes 12582912 | tf_op jit(solution)/shard_map/all_to_all | solution.py:60
  43.4 1.7 copy-start.2
  45.1 137.5 %collective-permute-start = (f32[16,1,1024]{2,0,1:T(8,128)S(1)}, f32[16,1,1024]{2,0,1:T(8,128)S(1)}, u32[]{:S(2)}, u32[]{:S(2)}) collective-permute-start(f32[16,1,1024]{2,0,1:T(8,128)S(1)} %get-tuple-element.10), channel_id=1, source_target_pairs={{0,8},{8,16},{16,24},{1,9},{9,17},{17,25},{2,10},{10,18},{18,26},{... | collective-permute-start | bytes 196616 | tf_op jit(solution)/shard_map/ppermute | solution.py:15
  49.7 132.9 %collective-permute-start.1 = (f32[16,1,1024]{2,0,1:T(8,128)S(1)}, f32[16,1,1024]{2,0,1:T(8,128)S(1)}, u32[]{:S(2)}, u32[]{:S(2)}) collective-permute-start(f32[16,1,1024]{2,0,1:T(8,128)S(1)} %get-tuple-element.9), channel_id=1, source_target_pairs={{8,0},{16,8},{24,16},{9,1},{17,9},{25,17},{10,2},{18,10},{26,18},{... | collective-permute-start | bytes 196616 | tf_op jit(solution)/shard_map/ppermute | solution.py:17
  160.5 22.1 %copy-start.3 = (f32[512,16]{0,1:T(8,128)S(1)}, f32[512,16]{0,1:T(8,128)}, u32[]{:S(2)}) copy-start(f32[512,16]{0,1:T(8,128)} %param.9) | copy-start | bytes 98308
  168.8 30.9 %slice-start = ((s8[6291456]{0:T(1024)(128)(4,1)}), s8[2097152]{0:T(1024)(128)(4,1)S(1)}, s32[]{:S(2)}) async-start(s8[6291456]{0:T(1024)(128)(4,1)} %bitcast.35), calls=%async_computation.2 | async-start | bytes 4194304
  170.2 3.4 collective-permute-start.2
  171.5 3.9 %collective-permute-start.3 = (bf16[512,48,1]{0,2,1:T(2,128)(2,1)S(1)}, bf16[512,48,1]{0,2,1:T(2,128)(2,1)S(1)}, u32[]{:S(2)}, u32[]{:S(2)}) collective-permute-start(bf16[512,48,1]{0,2,1:T(2,128)(2,1)S(1)} %get-tuple-element.8), channel_id=1, source_target_pairs={{1,0},{2,1},{3,2},{4,3},{5,4},{6,5},{7,6},{9,8},{10,9},{11,10},{12... | collective-permute-start | bytes 147464 | tf_op jit(solution)/shard_map/ppermute | solution.py:17
  176.5 23.2 %collective-permute-start.4 = (bf16[512,1,130]{0,2,1:T(8,128)(2,1)S(1)}, bf16[512,1,130]{0,2,1:T(8,128)(2,1)S(1)}, u32[]{:S(2)}, u32[]{:S(2)}) collective-permute-start(bf16[512,1,130]{0,2,1:T(8,128)(2,1)S(1)} %get-tuple-element.5), channel_id=1, source_target_pairs={{0,8},{8,16},{16,24},{1,9},{9,17},{17,25},{2,10},{10,18},{18,26},{... | collective-permute-start | bytes 399368 | tf_op jit(solution)/shard_map/ppermute | solution.py:15
  180.8 18.9 %slice-start.1 = ((s8[6291456]{0:T(1024)(128)(4,1)}), s8[4194304]{0:T(1024)(128)(4,1)S(1)}, s32[]{:S(2)}) async-start(s8[6291456]{0:T(1024)(128)(4,1)} %bitcast.35), calls=%async_computation.3 | async-start | bytes 8388608
  180.8 18.8 %collective-permute-start.5 = (bf16[512,1,130]{0,2,1:T(8,128)(2,1)S(1)}, bf16[512,1,130]{0,2,1:T(8,128)(2,1)S(1)}, u32[]{:S(2)}, u32[]{:S(2)}) collective-permute-start(bf16[512,1,130]{0,2,1:T(8,128)(2,1)S(1)} %get-tuple-element.6), channel_id=1, source_target_pairs={{8,0},{16,8},{24,16},{9,1},{17,9},{25,17},{10,2},{18,10},{26,18},{... | collective-permute-start | bytes 399368 | tf_op jit(solution)/shard_map/ppermute | solution.py:17
  199.6 6.4 %copy-start.4 = (f32[512]{0:T(512)S(1)}, f32[512]{0:T(512)}, u32[]{:S(2)}) copy-start(f32[512]{0:T(512)} %param.8) | copy-start | bytes 6148
  252.6 91.6 %copy-start.1 = (bf16[512,512]{1,0:T(8,128)(2,1)S(1)}, bf16[512,512]{1,0:T(8,128)(2,1)}, u32[]{:S(2)}) copy-start(bf16[512,512]{1,0:T(8,128)(2,1)} %param.7) | copy-start | bytes 1572868

commit v2 on v1

--- a/solution.py
+++ b/solution.py
@@ -48,26 +48,30 @@
 
 
 def local(modes_field, chaos_basis, node_weights, node_points, kl_fields, velocity):
-    columns = modes_field.shape[2] // lax.axis_size("mode")
+    parts = lax.axis_size("mode")
+    share, rows, width = modes_field.shape
+    columns = width // parts
     first_column = lax.axis_index("mode") * columns
     kl_rimmed = extended(kl_fields, (("grid", 1),), 1)
     kl_rimmed = jnp.pad(kl_rimmed, ((0, 0), (0, 0), (1, 1)))
     kl_piece = lax.dynamic_slice_in_dim(kl_rimmed, first_column, columns + 2, 2)
     velocity_piece = lax.dynamic_slice_in_dim(velocity, first_column, columns, 2)
-    result = jnp.einsum(
-        "qp,prc->qrc",
-        chaos_basis,
-        lax.all_to_all(modes_field, "mode", split_axis=2, concat_axis=0, tiled=True),
-        preferred_element_type=jnp.float32,
+    modes_rimmed = extended(modes_field, (("grid", 1),), 1)
+    outgoing = modes_rimmed.reshape(share, rows + 2, parts, columns).transpose(2, 0, 1, 3)
+    outgoing = outgoing.reshape(parts, share, (rows + 2) * columns)
+    incoming = lax.all_to_all(outgoing, "mode", split_axis=0, concat_axis=0, tiled=True)
+    incoming = incoming.reshape(parts * share, (rows + 2) * columns)
+    nodal = jnp.dot(chaos_basis, incoming, preferred_element_type=jnp.float32)
+    nodal = nodal.astype(jnp.bfloat16).reshape(-1, rows + 2, columns)
+    padded_field = extended(nodal, (("mode", 2),), 1)
+    weighted = node_terms(padded_field, kl_piece, node_points, velocity_piece, node_weights)
+    tendency = jnp.dot(
+        chaos_basis.T, weighted.reshape(-1, rows * columns), preferred_element_type=jnp.float32
     )
-    nodal = result.astype(jnp.bfloat16)
-    padded_field = extended(nodal, (("mode", 2), ("grid", 1)), 1)
-    weighted = node_terms(padded_field, kl_piece, node_points, velocity_piece, node_weights)
-    tendency = jnp.einsum(
-        "qp,qrc->prc", chaos_basis, weighted, preferred_element_type=jnp.float32
-    )
-    tendency = tendency.astype(jnp.bfloat16)
-    return lax.all_to_all(tendency, "mode", split_axis=0, concat_axis=2, tiled=True)
+    tendency = tendency.astype(jnp.bfloat16).reshape(parts, share, rows * columns)
+    back = lax.all_to_all(tendency, "mode", split_axis=0, concat_axis=0, tiled=True)
+    back = back.reshape(parts, share, rows, columns).transpose(1, 2, 0, 3)
+    return back.reshape(share, rows, width)
 
 
 def solution(mesh):

time: 346 us -> 323 us (0.934)
  other arithmetic: 16.4 us -> 70.2 us
  matrix products: 73 us -> 29.4 us
  local copies, waits for them, and re-layouts: 94.7 us -> 59.8 us
    unnamed x18 -> x14, local copies, waits for them, and re-layouts: 53.3 us -> 7.39 us
    convert_element_type x1, other arithmetic: 8.26 us -> 53.9 us  [node_terms(): return (node_weights[:, None, None] * flux).astype(jnp.bfloat16)]
    reshape x0 -> x4, local copies, waits for them, and re-layouts: none -> 43 us  [the longest x1 11.4 us: local(): modes_rimmed.reshape(share, rows + 2, parts, columns).transpose(2, 0, 1, 3)]
    dot_general x1 -> x2, matrix products: 46.6 us -> 13.4 us  [the longest x1 6.89 us: local(): nodal = jnp.dot(chaos_basis, incoming, preferred_element_type=jnp.float32)]
    all_to_all x3 -> x0, local copies, waits for them, and re-layouts: 30.9 us -> none  [the longest x2 26.3 us: local(): lax.all_to_all(modes_field, 'mode', split_axis=2, concat_axis=0, tiled=True)]
    unnamed x1 -> x0, matrix products: 9.32 us -> none
    convert_element_type x1 -> x0, local copies, waits for them, and re-layouts: 9.17 us -> none  [local(): tendency = tendency.astype(jnp.bfloat16)]
    concatenate x0 -> x1, other arithmetic: none -> 7.94 us  [extended(): jnp.concatenate([lax.ppermute(tail, axis, [(i, (i + 1) % count) for i in...]
  transfers between devices with their start and end apart: 7 -> 7, of which waited for: 2 -> 3; matrix products, arithmetic and copies ran while one was open for 24% -> 9% of each run, Pallas kernels for 0% -> 0%
where the time goes in v2:
time: 323 us; the launch traced here: 322 us
  blocking collectives  77 us (24%)
  other arithmetic  70.2 us (22%)
  waiting for transfers between devices  64.4 us (20%)
  local copies, waits for them, and re-layouts  59.8 us (19%)
  matrix products  29.4 us (9%)
  starting transfers between devices  20.7 us (6%)
    all_to_all x1, blocking collectives, local(): lax.all_to_all(tendency, 'mode', split_axis=0, concat_axis=0, tiled=True)  77 us
    all_to_all x1, waiting for transfers between devices, local(): lax.all_to_all(outgoing, 'mode', split_axis=0, concat_axis=0, tiled=True)  61.9 us
    convert_element_type x1, other arithmetic, node_terms(): return (node_weights[:, None, None] * flux).astype(jnp.bfloat16)  53.9 us
    dot_general x1, matrix products, node_terms(): jnp.einsum('qk,krc->qrc', node_points, kl_piece, precision=lax.Precision....  16 us
    ppermute x3, starting transfers between devices, extended(): lax.ppermute(tail, axis, [(i, (i + 1) % count) for i in range(ends)])  11.9 us
    reshape x1, local copies, waits for them, and re-layouts, local(): modes_rimmed.reshape(share, rows + 2, parts, columns).transpose(2, 0, 1, 3)  11.4 us
    reshape x1, local copies, waits for them, and re-layouts, local(): outgoing = outgoing.reshape(parts, share, (rows + 2) * columns)  11.4 us
    reshape x1, local copies, waits for them, and re-layouts, local(): return back.reshape(share, rows, width)  10.3 us
  transfers between devices with their start and end apart: 7, of which 3 were waited for; matrix products, arithmetic and copies ran while one was open for 9% of the time, Pallas kernels for 0%

profile of v2, /device:TPU:0, one launch (start us, length us, event | category | flops | bytes accessed | tf_op | source)
XLA Modules:
  0.0 321.7 jit_solution(14690333678127756293)
XLA Ops:
  0.0 0.0 copy-start
  0.0 2.0 fusion.40
  2.1 1.3 collective-permute-start.3
  3.5 5.6 %collective-permute-start.2 = (bf16[64,1,1024]{2,0,1:T(8,128)(2,1)S(1)}, bf16[64,1,1024]{2,0,1:T(8,128)(2,1)S(1)}, u32[]{:S(2)}, u32[]{:S(2)}) collective-permute-start(bf16[64,1,1024]{2,0,1:T(8,128)(2,1)S(1)} %copy.29), channel_id=1, source_target_pairs={{0,8},{8,16},{16,24},{1,9},{9,17},{17,25},{2,10},{10,18},{18,26},{... | collective-permute-start | bytes 393224 | tf_op jit(solution)/shard_map/ppermute | solution.py:15
  9.0 1.5 collective-permute-done.3
  10.5 0.2 copy.23
  10.7 1.0 collective-permute-done.2
  11.8 0.2 copy.22
  12.0 7.9 %pad_maximum_fusion = bf16[64,50,1024]{2,1,0:T(8,128)(2,1)} fusion(bf16[64,1,1024]{2,1,0:T(2,128)(2,1)S(1)} %copy.23, bf16[64,48,1024]{2,1,0:T(8,128)(2,1)} %param.6, bf16[64,1,1024]{2,1,0:T(2,128)(2,1)S(1)} %copy.22), kind=kLoop, calls=%fused_computation.21 | loop fusion | flops 19660800 | bytes 13107200 | tf_op jit(solution)/shard_map/concatenate | solution.py:13
  19.9 11.4 %reshape.34 = bf16[64,50,8,128]{3,2,1,0:T(8,128)(2,1)} reshape(bf16[64,50,1024]{2,1,0:T(8,128)(2,1)} %pad_maximum_fusion) | data formatting | bytes 13107200 | tf_op jit(solution)/shard_map/reshape | solution.py:60
  31.3 6.8 %copy.25 = bf16[8,64,50,128]{3,2,1,0:T(8,128)(2,1)} copy(bf16[8,64,50,128]{3,0,2,1:T(8,128)(2,1)} %bitcast.32) | data formatting | bytes 13107200 | tf_op jit(solution)/shard_map/transpose | solution.py:60
  38.1 11.4 %reshape.26 = bf16[8,64,6400]{2,1,0:T(8,128)(2,1)} reshape(bf16[8,64,50,128]{3,2,1,0:T(8,128)(2,1)} %copy.25) | data formatting | bytes 13107200 | tf_op jit(solution)/shard_map/reshape | solution.py:61
  49.5 4.8 %all-to-all-start = ((bf16[8,64,6400]{2,1,0:T(8,128)(2,1)}), bf16[8,64,6400]{2,1,0:T(8,128)(2,1)}, u32[]{:S(2)}, u32[]{:S(2)}) async-start(bf16[8,64,6400]{2,1,0:T(8,128)(2,1)} %reshape.26), calls=%async_computation | async-start | bytes 13107200 | tf_op jit(solution)/shard_map/all_to_all | solution.py:62
  54.3 0.0 copy-start.3
  54.3 3.7 %copy.17 = f32[16,48,1024]{2,0,1:T(8,128)S(1)} copy(f32[16,48,1024]{2,1,0:T(8,128)} %param.10) | data formatting | bytes 6291456 | tf_op args[4]
  58.0 0.0 copy-start.1
  58.0 1.7 copy-done.1
  59.7 1.3 collective-permute-start.1
  61.0 5.0 %collective-permute-start = (f32[16,1,1024]{2,0,1:T(8,128)S(1)}, f32[16,1,1024]{2,0,1:T(8,128)S(1)}, u32[]{:S(2)}, u32[]{:S(2)}) collective-permute-start(f32[16,1,1024]{2,0,1:T(8,128)S(1)} %get-tuple-element.10), channel_id=1, source_target_pairs={{0,8},{8,16},{16,24},{1,9},{9,17},{17,25},{2,10},{10,18},{18,26},{... | collective-permute-start | bytes 196616 | tf_op jit(solution)/shard_map/ppermute | solution.py:15
  66.0 0.8 fusion.33
  66.8 61.9 %all-to-all-done = bf16[8,64,6400]{2,1,0:T(8,128)(2,1)} async-done(((bf16[8,64,6400]{2,1,0:T(8,128)(2,1)}), bf16[8,64,6400]{2,1,0:T(8,128)(2,1)}, u32[]{:S(2)}, u32[]{:S(2)}) %all-to-all-start) | async-done | bytes 6553632 | tf_op jit(solution)/shard_map/all_to_all | solution.py:62
  128.7 0.0 copy-start.2
  128.7 0.0 copy-done
  128.7 6.9 %convolution_convert_fusion = bf16[6400,512]{1,0:T(8,128)(2,1)S(1)} fusion(bf16[512,6400]{1,0:T(8,128)(2,1)} %bitcast.4, bf16[512,512]{1,0:T(8,128)(2,1)S(1)} %copy-done), kind=kOutput, calls=%fused_computation.19 | convolution fusion | flops 3358720000 | bytes 13631488 | tf_op jit(solution)/shard_map/dot_general | solution.py:64
  135.6 0.2 fusion.39
  135.8 1.3 collective-permute-start.4
  137.1 1.5 collective-permute-start.5
  138.6 0.0 collective-permute-done.1
  138.6 0.0 collective-permute-done
  138.6 0.0 copy-done.3
  138.6 0.0 copy-done.2
  138.6 16.0 %exponential_bitcast_fusion = f32[512,50,130]{0,2,1:T(8,128)} fusion(s32[]{:T(128)S(6)} %select_n.6, f32[16,1,1024]{2,0,1:T(8,128)S(1)} %collective-permute-done, f32[16,48,1024]{2,0,1:T(8,128)S(1)} %copy-done.2, f32[16,1,1024]{2,0,1:T(8,128)S(1)} %collective-permute-done.1, f32[512,16]{0,1:T(8,128)S(1)} %copy-done.3), kind=kOutput, calls=%fused_computation | convolution fusion | flops 639912000 | bytes 16622592 | tf_op jit(solution)/shard_map/qk,krc->qrc/dot_general | solution.py:27
  154.6 0.0 copy-start.4
  154.6 0.0 collective-permute-done.4
  154.6 0.0 collective-permute-done.5
  154.6 7.5 %maximum_convert_fusion = f32[512,50,130]{0,2,1:T(8,128)} fusion(bf16[512,50,1]{0,2,1:T(2,128)(2,1)S(1)} %collective-permute-done.5, bf16[512,50,128]{0,2,1:T(8,128)(2,1)S(1)} %bitcast.37, bf16[512,50,1]{0,2,1:T(2,128)(2,1)S(1)} %collective-permute-done.4), kind=kLoop, calls=%fused_computation.22 | loop fusion | flops 19968000 | bytes 19968000 | tf_op jit(solution)/shard_map/convert_element_type | solution.py:25
  162.1 0.0 copy-done.4
  162.2 53.9 %fusion.5 = bf16[512,48,128]{0,2,1:T(8,128)(2,1)} fusion(f32[512,50,130]{0,2,1:T(8,128)} %exponential_bitcast_fusion, f32[512,50,130]{0,2,1:T(8,128)} %maximum_convert_fusion, f32[48,128]{1,0:T(8,128)S(1)} %get-tuple-element.12, f32[48,128]{1,0:T(8,128)S(1)} %get-tuple-element.11, f32[512]{0:T(512)S(1)} %copy-done.4), kind=kLoop, calls=%fused_computation.7 | loop fusion | flops 84934656 | bytes 132171776 | tf_op jit(solution)/shard_map/convert_element_type | solution.py:47
  216.1 6.5 %convolution_convert_fusion.1 = bf16[6144,512]{0,1:T(8,128)(2,1)S(1)} fusion(bf16[512,6144]{0,1:T(8,128)(2,1)} %bitcast.39, bf16[512,512]{1,0:T(8,128)(2,1)S(1)} %copy-done), kind=kOutput, calls=%fused_computation.20 | convolution fusion | flops 3224371200 | bytes 13107200 | tf_op jit(solution)/shard_map/dot_general | solution.py:68
  222.6 77.0 %all_to_all.10 = bf16[8,64,6144]{2,1,0:T(8,128)(2,1)S(1)} all-to-all(bf16[8,64,6144]{2,1,0:T(8,128)(2,1)S(1)} %bitcast.38), channel_id=1, replica_groups=mesh['grid'=4,'mode'=8] {'mode'}, dimensions={0} | all-to-all | bytes 12582912 | tf_op jit(solution)/shard_map/all_to_all | solution.py:72
  299.6 1.9 copy.31
  301.5 10.0 %copy.33 = bf16[8,64,48,128]{3,0,2,1:T(8,128)(2,1)} copy(bf16[8,64,48,128]{3,2,1,0:T(8,128)(2,1)S(1)} %bitcast.34) | data formatting | bytes 12582912 | tf_op jit(solution)/shard_map/reshape | solution.py:73
  311.5 10.3 %reshape.32 = bf16[64,48,1024]{2,1,0:T(8,128)(2,1)} reshape(bf16[64,48,8,128]{3,2,1,0:T(8,128)(2,1)} %bitcast.35) | data formatting | bytes 12582912 | tf_op jit(solution)/shard_map/reshape | solution.py:74
  (3 shorter events, 0.1 us)
Async XLA Ops:
  0.0 128.7 %copy-start = (bf16[512,512]{1,0:T(8,128)(2,1)S(1)}, bf16[512,512]{1,0:T(8,128)(2,1)}, u32[]{:S(2)}) copy-start(bf16[512,512]{1,0:T(8,128)(2,1)} %param.7) | copy-start | bytes 1572868
  2.1 8.4 %collective-permute-start.3 = (bf16[64,1,1024]{2,0,1:T(8,128)(2,1)S(1)}, bf16[64,1,1024]{2,0,1:T(8,128)(2,1)S(1)}, u32[]{:S(2)}, u32[]{:S(2)}) collective-permute-start(bf16[64,1,1024]{2,0,1:T(8,128)(2,1)S(1)} %copy.30), channel_id=1, source_target_pairs={{8,0},{16,8},{24,16},{9,1},{17,9},{25,17},{10,2},{18,10},{26,18},{... | collective-permute-start | bytes 393224 | tf_op jit(solution)/shard_map/ppermute | solution.py:17
  3.5 8.3 %collective-permute-start.2 = (bf16[64,1,1024]{2,0,1:T(8,128)(2,1)S(1)}, bf16[64,1,1024]{2,0,1:T(8,128)(2,1)S(1)}, u32[]{:S(2)}, u32[]{:S(2)}) collective-permute-start(bf16[64,1,1024]{2,0,1:T(8,128)(2,1)S(1)} %copy.29), channel_id=1, source_target_pairs={{0,8},{8,16},{16,24},{1,9},{9,17},{17,25},{2,10},{10,18},{18,26},{... | collective-permute-start | bytes 393224 | tf_op jit(solution)/shard_map/ppermute | solution.py:15
  49.5 79.2 %all-to-all-start = ((bf16[8,64,6400]{2,1,0:T(8,128)(2,1)}), bf16[8,64,6400]{2,1,0:T(8,128)(2,1)}, u32[]{:S(2)}, u32[]{:S(2)}) async-start(bf16[8,64,6400]{2,1,0:T(8,128)(2,1)} %reshape.26), calls=%async_computation | async-start | bytes 13107200 | tf_op jit(solution)/shard_map/all_to_all | solution.py:62
  54.3 84.3 %copy-start.3 = (f32[512,16]{0,1:T(8,128)S(1)}, f32[512,16]{0,1:T(8,128)}, u32[]{:S(2)}) copy-start(f32[512,16]{0,1:T(8,128)} %param.9) | copy-start | bytes 98308
  58.0 1.7 copy-start.1
  59.7 78.9 %collective-permute-start.1 = (f32[16,1,1024]{2,0,1:T(8,128)S(1)}, f32[16,1,1024]{2,0,1:T(8,128)S(1)}, u32[]{:S(2)}, u32[]{:S(2)}) collective-permute-start(f32[16,1,1024]{2,0,1:T(8,128)S(1)} %get-tuple-element.9), channel_id=1, source_target_pairs={{8,0},{16,8},{24,16},{9,1},{17,9},{25,17},{10,2},{18,10},{26,18},{... | collective-permute-start | bytes 196616 | tf_op jit(solution)/shard_map/ppermute | solution.py:17
  61.0 77.6 %collective-permute-start = (f32[16,1,1024]{2,0,1:T(8,128)S(1)}, f32[16,1,1024]{2,0,1:T(8,128)S(1)}, u32[]{:S(2)}, u32[]{:S(2)}) collective-permute-start(f32[16,1,1024]{2,0,1:T(8,128)S(1)} %get-tuple-element.10), channel_id=1, source_target_pairs={{0,8},{8,16},{16,24},{1,9},{9,17},{17,25},{2,10},{10,18},{18,26},{... | collective-permute-start | bytes 196616 | tf_op jit(solution)/shard_map/ppermute | solution.py:15
  128.7 9.9 %copy-start.2 = (f32[16,48,1024]{2,0,1:T(8,128)S(1)}, f32[16,48,1024]{2,0,1:T(8,128)}, u32[]{:S(2)}) copy-start(f32[16,48,1024]{2,0,1:T(8,128)} %copy-done.1) | copy-start | bytes 9437188
  135.8 18.8 %collective-permute-start.4 = (bf16[512,50,1]{0,2,1:T(2,128)(2,1)S(1)}, bf16[512,50,1]{0,2,1:T(2,128)(2,1)S(1)}, u32[]{:S(2)}, u32[]{:S(2)}) collective-permute-start(bf16[512,50,1]{0,2,1:T(2,128)(2,1)S(1)} %get-tuple-element.5), channel_id=1, source_target_pairs={{0,1},{1,2},{2,3},{3,4},{4,5},{5,6},{6,7},{8,9},{9,10},{10,11},{11... | collective-permute-start | bytes 153608 | tf_op jit(solution)/shard_map/ppermute | solution.py:15
  137.1 17.5 %collective-permute-start.5 = (bf16[512,50,1]{0,2,1:T(2,128)(2,1)S(1)}, bf16[512,50,1]{0,2,1:T(2,128)(2,1)S(1)}, u32[]{:S(2)}, u32[]{:S(2)}) collective-permute-start(bf16[512,50,1]{0,2,1:T(2,128)(2,1)S(1)} %get-tuple-element.6), channel_id=1, source_target_pairs={{1,0},{2,1},{3,2},{4,3},{5,4},{6,5},{7,6},{9,8},{10,9},{11,10},{12... | collective-permute-start | bytes 153608 | tf_op jit(solution)/shard_map/ppermute | solution.py:17
  154.6 7.6 %copy-start.4 = (f32[512]{0:T(512)S(1)}, f32[512]{0:T(512)}, u32[]{:S(2)}) copy-start(f32[512]{0:T(512)} %param.8) | copy-start | bytes 6148
